TPU v7x, 512 devices: a whole 4x8x8 slice. The times are simulated.
512 devices in a mesh: dp: 8 (over y_hi, x), expert: 64 (over y_lo, z, core).
Axes of the slice: x: 4, y: 8 (y_hi: 2, y_lo: 4; y = y_hi * 4 + y_lo), z: 8, core: 2. Of those that a mesh axis runs over, the one named last changes fastest.
Arguments:
- tokens: bfloat16 [8192, 2560], P(('dp', 'expert')), may hold values from -6 to 6
- grad_out: bfloat16 [8192, 2560], P(('dp', 'expert')), may hold values from -6 to 6
- expert_ids: int32 [8192, 2], P(('dp', 'expert')), may hold values from 0 to 63, as said below
- gates: bfloat16 [8192, 2], P(('dp', 'expert')), may hold values from 0.099609375 to 1
- w_gate: bfloat16 [64, 2560, 1024], P('expert', None, 'dp'), may hold values from -0.125 to 0.125
- w_up: bfloat16 [64, 2560, 1024], P('expert', None, 'dp'), may hold values from -0.125 to 0.125
- w_down: bfloat16 [64, 1024, 2560], P('expert', 'dp'), may hold values from -0.1875 to 0.1875
Outputs:
- out_tokens: bfloat16 [8192, 2560], P(('dp', 'expert'))
- grad_tokens: bfloat16 [8192, 2560], P(('dp', 'expert'))
- grad_gate: bfloat16 [64, 2560, 1024], P('expert', None, 'dp')
- grad_up: bfloat16 [64, 2560, 1024], P('expert', None, 'dp')
- grad_down: bfloat16 [64, 1024, 2560], P('expert', 'dp')
Inputs may be any that keep to these rules, and one draw needn't show every extreme that they name: `expert_ids`: each token names 2 different experts. Over the tokens of all devices at one index of expert taken together, one expert, the same at every index, is named exactly 8 times; a second one, also the same at every index, exactly 5 times; every other expert at most 5 times.
All inputs are finite; a program needn't handle non-finite values.
Results may differ from a plain program's by a relative error of at most 0.019.
Values may be sent and summed in bfloat16 or wider, within the bound.
No kernel may reach another device: no remote copies, remote signals or barrier semaphores. Data moves between devices by JAX's collectives and lax.ppermute only.
A program may use at most 128 MiB of HBM per device.

v0:
```python
import jax
import jax.numpy as jnp
from jax import lax
from jax.sharding import PartitionSpec as P


def expert_rows(rows_in, cot_in, gate_weight, up_weight, down_weight):
    gate_pre = jnp.dot(rows_in, gate_weight, preferred_element_type=jnp.float32)
    up_pre = jnp.dot(rows_in, up_weight, preferred_element_type=jnp.float32)
    hidden = (jax.nn.silu(gate_pre) * up_pre).astype(jnp.bfloat16)
    partial_value = jnp.dot(hidden, down_weight, preferred_element_type=jnp.float32).astype(
        jnp.bfloat16
    )
    first_dim = (((0,), (0,)), ((), ()))
    last_dim = (((1,), (1,)), ((), ()))
    grad_down = lax.dot_general(hidden, cot_in, first_dim, preferred_element_type=jnp.float32)
    d_hidden = lax.dot_general(cot_in, down_weight, last_dim, preferred_element_type=jnp.float32)
    sig = jax.nn.sigmoid(gate_pre)
    d_gate = (d_hidden * up_pre * sig * (1.0 + gate_pre * (1.0 - sig))).astype(jnp.bfloat16)
    d_up = (d_hidden * gate_pre * sig).astype(jnp.bfloat16)
    grad_gate = lax.dot_general(rows_in, d_gate, first_dim, preferred_element_type=jnp.float32)
    grad_up = lax.dot_general(rows_in, d_up, first_dim, preferred_element_type=jnp.float32)
    back_term = lax.dot_general(d_gate, gate_weight, last_dim, preferred_element_type=jnp.float32)
    back_term = (
        back_term + lax.dot_general(d_up, up_weight, last_dim, preferred_element_type=jnp.float32)
    ).astype(jnp.bfloat16)
    return (partial_value, back_term, grad_gate, grad_up, grad_down)


def collect_slots(values, slot_index, weights):
    taken = jnp.take(values, slot_index.reshape(-1), axis=0, mode="fill", fill_value=0)
    taken = taken.reshape(slot_index.shape[0], slot_index.shape[1], values.shape[1]).astype(
        jnp.float32
    )
    if weights is None:
        return jnp.sum(taken, axis=1)
    return jnp.sum(weights.astype(jnp.float32)[:, :, None] * taken, axis=1)


def body(tokens, grad_out, expert_ids, gates, w_gate, w_up, w_down):
    dp_count = lax.axis_size("dp")
    experts = lax.axis_size("expert")
    local_rows = tokens.shape[0]
    width = tokens.shape[1]
    top_count = expert_ids.shape[1]
    group_rows = dp_count * local_rows
    assigned = group_rows * top_count
    mean_slots = assigned // experts
    cap_hot = 2 * mean_slots
    side = 128
    extra = jnp.concatenate(
        [
            expert_ids.astype(jnp.bfloat16),
            gates,
            jnp.zeros((local_rows, side - 2 * top_count), jnp.bfloat16),
        ],
        axis=1,
    )
    packed = jnp.concatenate([tokens, grad_out, extra], axis=1)
    group = lax.all_gather(packed, "dp", axis=0, tiled=True)
    group_tokens = group[:, :width]
    group_grads = group[:, width : 2 * width]
    group_ids = group[:, 2 * width : 2 * width + top_count].astype(jnp.int32)
    group_gates = group[:, 2 * width + top_count : 2 * width + 2 * top_count]
    flat_ids = group_ids.reshape(-1)
    expert_range = jnp.arange(experts, dtype=jnp.int32)
    member = (flat_ids[:, None] == expert_range[None, :]).astype(jnp.int32)
    before = jnp.sum((jnp.cumsum(member, axis=0) - member) * member, axis=1)
    slot_count = experts * cap_hot
    slot_of = (flat_ids * cap_hot + before).astype(jnp.int32)
    owner = jnp.full((slot_count,), assigned, jnp.int32)
    owner = owner.at[slot_of].set(jnp.arange(assigned, dtype=jnp.int32), mode="drop")
    filled = owner < assigned
    safe = jnp.where(filled, owner, 0)
    tok = safe // top_count
    gate_of = jnp.where(filled, group_gates.reshape(-1)[safe].astype(jnp.float32), 0.0)
    rows_taken = jnp.where(filled[:, None], group_tokens[tok], jnp.zeros((), jnp.bfloat16))
    cot_taken = (gate_of[:, None] * group_grads[tok].astype(jnp.float32)).astype(jnp.bfloat16)
    send = jnp.concatenate([rows_taken, cot_taken], axis=1)
    arrived = lax.all_to_all(
        send.reshape(experts, cap_hot, 2 * width), "expert", 0, 0, tiled=True
    ).reshape(slot_count, 2 * width)
    partial_value, back_term, grad_gate, grad_up, grad_down = expert_rows(
        arrived[:, :width], arrived[:, width:], w_gate[0], w_up[0], w_down[0]
    )
    ret = jnp.concatenate([partial_value, back_term], axis=1)
    returned = lax.all_to_all(
        ret.reshape(experts, cap_hot, 2 * width), "expert", 0, 0, tiled=True
    ).reshape(slot_count, 2 * width)
    slot_pairs = slot_of.reshape(group_rows, top_count)
    out_part = collect_slots(returned[:, :width], slot_pairs, group_gates)
    back_part = collect_slots(returned[:, width:], slot_pairs, None)
    both = jnp.concatenate([out_part, back_part], axis=1).astype(jnp.bfloat16)
    spread = lax.all_to_all(both.reshape(dp_count, local_rows, 2 * width), "dp", 0, 0, tiled=True)
    total = jnp.sum(spread.astype(jnp.float32), axis=0).astype(jnp.bfloat16)
    return (
        total[:, :width],
        total[:, width:],
        grad_gate.astype(jnp.bfloat16)[None],
        grad_up.astype(jnp.bfloat16)[None],
        grad_down.astype(jnp.bfloat16)[None],
    )


def solution(mesh):
    in_specs = (
        P(("dp", "expert"), None),
        P(("dp", "expert"), None),
        P(("dp", "expert"), None),
        P(("dp", "expert"), None),
        P("expert", None, "dp"),
        P("expert", None, "dp"),
        P("expert", "dp", None),
    )
    out_specs = (
        P(("dp", "expert"), None),
        P(("dp", "expert"), None),
        P("expert", None, "dp"),
        P("expert", None, "dp"),
        P("expert", "dp", None),
    )
    return jax.shard_map(body, mesh=mesh, in_specs=in_specs, out_specs=out_specs, check_vma=False)
```

profile of v0, /device:TPU:56, one launch (start us, length us, event | category | flops | bytes accessed | tf_op | source)
XLA Modules:
  0.0 495.1 jit_solution(2697792149016737092)
XLA Ops:
  7.2 0.7 convert_element_type.70
  8.1 0.7 copy.18
  8.8 1.7 concatenate.19
  10.5 70.9 %all-gather.2.cloned.1.call-done = bf16[128,5248]{1,0:T(8,128)(2,1)} async-done(((bf16[16,5248]{1,0:T(8,128)(2,1)}), bf16[128,5248]{1,0:T(8,128)(2,1)}) %all-gather.2.cloned.1.call-update) | async-done | bytes 1343504 | tf_op jit(solution)/shard_map/all_gather | solution.py:60
  81.4 1.0 slice_convert_fusion.1
  82.4 0.1 eq.25
  82.5 0.1 eq.29
  82.7 0.8 broadcast_multiply_fusion
  83.5 0.1 mul.70
  83.6 0.6 reduce-window.6
  84.2 0.2 slice_reduce_fusion
  84.5 0.1 fusion.22
  84.6 1.4 scatter_custom_fusion
  86.1 0.1 reshape.105
  86.3 3.4 gather_fusion.1
  89.9 3.5 gather_fusion.2
  93.4 3.5 gather_fusion
  96.8 2.4 fusion
  99.2 0.1 copy-done.3
  99.4 0.2 bitcast_select_fusion
  99.6 0.8 pad_maximum_fusion
  100.4 144.5 %all_to_all.15 = bf16[64,8,5120]{2,1,0:T(8,128)(2,1)S(1)} all-to-all(bf16[64,8,5120]{2,1,0:T(8,128)(2,1)S(1)} %pad_maximum_fusion), channel_id=1, replica_groups=mesh['dp'=8,'expert'=64] {'expert'}, dimensions={0} | all-to-all | bytes 10485760 | tf_op jit(solution)/shard_map/all_to_all | solution.py:80
  244.9 0.8 fusion.5
  245.7 0.7 copy-done.6
  246.4 0.8 fusion.11
  247.3 0.9 multiply_convert_fusion.2
  248.2 0.8 convolution_convert_fusion
  249.0 0.8 fusion.17
  249.9 0.9 add_convert_fusion
  250.8 3.1 maximum_bitcast_fusion
  253.9 14.9 %all-to-all-start.1 = ((bf16[64,8,5120]{2,1,0:T(8,128)(2,1)}), bf16[64,8,5120]{2,1,0:T(8,128)(2,1)}, u32[]{:S(2)}, u32[]{:S(2)}) async-start(bf16[64,8,5120]{2,1,0:T(8,128)(2,1)} %maximum_bitcast_fusion), calls=%async_computation.1 | async-start | bytes 10485760 | tf_op jit(solution)/shard_map/all_to_all | solution.py:87
  268.8 146.7 %all-to-all-done.1 = bf16[64,8,5120]{2,1,0:T(8,128)(2,1)} async-done(((bf16[64,8,5120]{2,1,0:T(8,128)(2,1)}), bf16[64,8,5120]{2,1,0:T(8,128)(2,1)}, u32[]{:S(2)}, u32[]{:S(2)}) %all-to-all-start.1) | async-done | bytes 5242912 | tf_op jit(solution)/shard_map/all_to_all | solution.py:87
  415.6 4.4 fusion.28
  420.0 5.9 %gather_fusion.3 = bf16[256,2560]{1,0:T(8,128)(2,1)} fusion(bf16[512,2560]{1,0:T(8,128)(2,1)} %get-tuple-element.10, s32[1024]{0:T(1024)S(1)} %pad_clamp_fusion), kind=kCustom, calls=%fused_computation.clone | custom fusion | bytes 2622464 | tf_op jit(solution)/shard_map/jit(_take)/gather | solution.py:31
  425.9 2.5 gather_fusion.4
  428.4 3.9 select_convert_fusion
  432.3 3.2 reshape.110
  435.6 4.0 convert_element_type.86
  439.5 5.3 %reduce.1 = bf16[128,2560]{1,0:T(8,128)(2,1)} reduce(bf16[128,2,2560]{2,1,0:T(2,128)(2,1)} %convert_element_type.86, bf16[]{:T(256)} %constant.21.clone.1), dimensions={1}, to_apply=%region_5.7.clone | reduce | flops 327680 | bytes 1966082 | tf_op jit(solution)/shard_map/reduce_sum | solution.py:36
  444.9 3.7 multiply_reduce_fusion
  448.5 1.2 pad_maximum_fusion.1
  449.8 9.2 %all-to-all-start.2 = ((bf16[8,16,5120]{2,1,0:T(8,128)(2,1)}), bf16[8,16,5120]{2,1,0:T(8,128)(2,1)S(1)}, u32[]{:S(2)}, u32[]{:S(2)}) async-start(bf16[8,16,5120]{2,1,0:T(8,128)(2,1)} %pad_maximum_fusion.1), calls=%async_computation.2 | async-start | bytes 2621440 | tf_op jit(solution)/shard_map/all_to_all | solution.py:94
  458.9 3.3 fusion.3
  462.2 3.6 fusion.1
  465.8 1.7 fusion.2
  467.6 19.8 %all-to-all-done.2 = bf16[8,16,5120]{2,1,0:T(8,128)(2,1)S(1)} async-done(((bf16[8,16,5120]{2,1,0:T(8,128)(2,1)}), bf16[8,16,5120]{2,1,0:T(8,128)(2,1)S(1)}, u32[]{:S(2)}, u32[]{:S(2)}) %all-to-all-start.2) | async-done | bytes 1310752 | tf_op jit(solution)/shard_map/all_to_all | solution.py:94
  487.4 0.2 reduce_sum.45
  487.6 0.7 fusion.30
  (46 shorter events, 0.6 us)
Async XLA Ops:
  7.2 240.1 %copy-start = (bf16[1,2560,128]{2,1,0:T(8,128)(2,1)S(1)}, bf16[1,2560,128]{2,1,0:T(8,128)(2,1)}, u32[]{:S(2)}) copy-start(bf16[1,2560,128]{2,1,0:T(8,128)(2,1)} %param.14) | copy-start | bytes 1966084
  7.2 74.2 %all-gather.2.cloned.1.call-start = ((), (), s32[]{:S(2)}) async-start(), calls=%async_computation.3 | async-start | bytes 1511424 | tf_op jit(solution)/shard_map/all_gather | solution.py:60
  81.4 8.4 %copy-start.5 = (bf16[128,5248]{1,0:T(8,128)(2,1)S(1)}, bf16[128,5248]{1,0:T(8,128)(2,1)}, u32[]{:S(2)}) copy-start(bf16[128,5248]{1,0:T(8,128)(2,1)} %all-gather.2.cloned.1.call-done) | copy-start | bytes 4030468
  96.8 2.5 copy-start.3
  100.4 144.5 %copy-start.7 = (bf16[1,128,2560]{2,1,0:T(8,128)(2,1)S(1)}, bf16[1,128,2560]{2,1,0:T(8,128)(2,1)}, u32[]{:S(2)}) copy-start(bf16[1,128,2560]{2,1,0:T(8,128)(2,1)} %param.15) | copy-start | bytes 1966084
  244.9 2.4 copy-start.2
  244.9 1.5 copy-start.6
  248.2 1.7 copy-start.10
  248.2 1.7 copy-start.8
  253.9 161.7 %all-to-all-start.1 = ((bf16[64,8,5120]{2,1,0:T(8,128)(2,1)}), bf16[64,8,5120]{2,1,0:T(8,128)(2,1)}, u32[]{:S(2)}, u32[]{:S(2)}) async-start(bf16[64,8,5120]{2,1,0:T(8,128)(2,1)} %maximum_bitcast_fusion), calls=%async_computation.1 | async-start | bytes 10485760 | tf_op jit(solution)/shard_map/all_to_all | solution.py:87
  444.9 3.7 copy-start.4
  449.8 12.4 %copy-start.11 = (bf16[512,128]{1,0:T(8,128)(2,1)S(1)}, bf16[512,128]{1,0:T(8,128)(2,1)}, u32[]{:S(2)}) copy-start(bf16[512,128]{1,0:T(8,128)(2,1)} %copy-done.10) | copy-start | bytes 393220
  449.8 37.6 %all-to-all-start.2 = ((bf16[8,16,5120]{2,1,0:T(8,128)(2,1)}), bf16[8,16,5120]{2,1,0:T(8,128)(2,1)S(1)}, u32[]{:S(2)}, u32[]{:S(2)}) async-start(bf16[8,16,5120]{2,1,0:T(8,128)(2,1)} %pad_maximum_fusion.1), calls=%async_computation.2 | async-start | bytes 2621440 | tf_op jit(solution)/shard_map/all_to_all | solution.py:94
  458.9 6.8 %slice-start = ((s8[5242880]{0:T(1024)(128)(4,1)}), s8[4194304]{0:T(1024)(128)(4,1)S(1)}, s32[]{:S(2)}) async-start(s8[5242880]{0:T(1024)(128)(4,1)} %bitcast.67), calls=%async_computation.4 | async-start | bytes 8388608
  462.2 3.6 slice-start.1
  462.2 3.6 copy-start.9
  465.8 22.5 %copy-start.1 = (bf16[1,2560,128]{2,1,0:T(8,128)(2,1)S(1)}, bf16[1,2560,128]{2,1,0:T(8,128)(2,1)}, u32[]{:S(2)}) copy-start(bf16[1,2560,128]{2,1,0:T(8,128)(2,1)} %param.14) | copy-start | bytes 1966084
Sparse Core Ops, SparseCore 0:
  11.8 69.6 all-gather.1
where the time goes:
time: 496 us; the launch traced here: 495 us
  waiting for transfers between devices  237 us (48%)
  blocking collectives  145 us (29%)
  local copies, waits for them, and re-layouts  36.8 us (7%)
  other arithmetic  24.2 us (5%)
  starting transfers between devices  24.1 us (5%)
  between operations  14.3 us (3%)
  matrix products  13.7 us (3%)
    all_to_all x1, waiting for transfers between devices, body(): lax.all_to_all(ret.reshape(experts, cap_hot, 2 * width), 'expert', 0, 0,...  147 us
    all_to_all x1, blocking collectives, body(): lax.all_to_all(send.reshape(experts, cap_hot, 2 * width), 'expert', 0, 0,...  145 us
    all_gather x1, waiting for transfers between devices, body(): group = lax.all_gather(packed, 'dp', axis=0, tiled=True)  70.9 us
    all_to_all x1, waiting for transfers between devices, body(): lax.all_to_all(both.reshape(dp_count, local_rows, 2 * width), 'dp', 0, 0,...  19.8 us
    all_to_all x1, starting transfers between devices, body(): lax.all_to_all(ret.reshape(experts, cap_hot, 2 * width), 'expert', 0, 0,...  14.9 us
  transfers between devices with their start and end apart: 3, of which 3 were waited for; matrix products, arithmetic and copies ran while one was open for 2% of the time, Pallas kernels for 0%

commit v1 on v0

--- a/solution.py
+++ b/solution.py
@@ -1,7 +1,21 @@
+import functools
 import jax
 import jax.numpy as jnp
 from jax import lax
 from jax.sharding import PartitionSpec as P
+from jax.lax import all_to_all, axis_size
+
+
+def serve_works_by_axis(row_data, array_axis):
+    return jnp.concatenate(
+        all_to_all(
+            jnp.stack([row_data] * axis_size("dp")), axis_name="dp", split_axis=0, concat_axis=0
+        ),
+        axis=array_axis,
+    )
+
+
+choose_the_zone = functools.partial(serve_works_by_axis, array_axis=0)
 
 
 def expert_rows(rows_in, cot_in, gate_weight, up_weight, down_weight):
@@ -57,7 +71,7 @@
         axis=1,
     )
     packed = jnp.concatenate([tokens, grad_out, extra], axis=1)
-    group = lax.all_gather(packed, "dp", axis=0, tiled=True)
+    group = choose_the_zone(packed)
     group_tokens = group[:, :width]
     group_grads = group[:, width : 2 * width]
     group_ids = group[:, 2 * width : 2 * width + top_count].astype(jnp.int32)

time: 496 us -> 450 us (0.907)
  waiting for transfers between devices: 237 us -> 167 us
  blocking collectives: 145 us -> 187 us
  between operations: 14.3 us -> 0.95 us
    all_gather x1 -> x0, waiting for transfers between devices: 70.9 us -> none  [body(): group = lax.all_gather(packed, 'dp', axis=0, tiled=True)]
    all_to_all x0 -> x1, blocking collectives: none -> 28 us  [serve_works_by_axis(): all_to_all(jnp.stack([row_data] * axis_size('dp')), axis_name='dp', split...]
    all_to_all x1, blocking collectives: 145 us -> 159 us  [body(): lax.all_to_all(send.reshape(experts, cap_hot, 2 * width), 'expert', 0, 0,...]
  transfers between devices with their start and end apart: 3 -> 2, of which waited for: 3 -> 2; matrix products, arithmetic and copies ran while one was open for 2% -> 2% of each run, Pallas kernels for 0% -> 0%
where the time goes in v1:
time: 450 us
  blocking collectives  187 us (42%)
  waiting for transfers between devices  167 us (37%)
  local copies, waits for them, and re-layouts  36.3 us (8%)
  starting transfers between devices  22.8 us (5%)
  other arithmetic  22.6 us (5%)
  matrix products  13.6 us (3%)
    all_to_all x1, blocking collectives, body(): lax.all_to_all(send.reshape(experts, cap_hot, 2 * width), 'expert', 0, 0,...  159 us
    all_to_all x1, waiting for transfers between devices, body(): lax.all_to_all(ret.reshape(experts, cap_hot, 2 * width), 'expert', 0, 0,...  147 us
    all_to_all x1, blocking collectives, serve_works_by_axis(): all_to_all(jnp.stack([row_data] * axis_size('dp')), axis_name='dp', split...  28 us
    all_to_all x1, waiting for transfers between devices, body(): lax.all_to_all(both.reshape(dp_count, local_rows, 2 * width), 'dp', 0, 0,...  19.8 us
    all_to_all x1, starting transfers between devices, body(): lax.all_to_all(ret.reshape(experts, cap_hot, 2 * width), 'expert', 0, 0,...  14.9 us
  transfers between devices with their start and end apart: 2, of which 2 were waited for; matrix products, arithmetic and copies ran while one was open for 2% of the time, Pallas kernels for 0%

profile of v1, /device:TPU:56, one launch (start us, length us, event | category | flops | bytes accessed | tf_op | source)
XLA Modules:
  0.0 449.5 jit_solution(5705340264516507835)
XLA Ops:
  0.6 0.7 convert_element_type.70
  1.4 0.1 copy.17
  1.5 0.7 copy.18
  2.2 1.0 concatenate.19
  3.4 28.0 %all_to_all.20 = bf16[8,16,5248]{2,1,0:T(8,128)(2,1)S(1)} all-to-all(bf16[8,16,5248]{2,1,0:T(8,128)(2,1)S(1)} %stack.2), channel_id=1, replica_groups=mesh['dp'=8,'expert'=64] {'dp'}, dimensions={0} | all-to-all | bytes 2686976 | tf_op jit(solution)/shard_map/all_to_all | solution.py:11
  31.5 0.1 eq.25
  31.7 0.1 eq.29
  31.8 0.1 mul.70
  32.0 0.6 reduce-window.6
  32.6 0.2 slice_reduce_fusion
  32.8 0.1 fusion.22
  33.0 1.4 scatter_custom_fusion
  34.4 0.1 broadcast_in_dim.56
  34.5 0.1 reshape.111
  34.7 3.4 gather_fusion.1
  38.1 3.5 gather_fusion.2
  41.6 3.5 gather_fusion
  45.1 2.4 fusion
  47.5 0.1 copy-done.3
  47.7 0.2 bitcast_select_fusion
  47.9 0.8 pad_maximum_fusion
  48.7 158.7 %all_to_all.21 = bf16[64,8,5120]{2,1,0:T(8,128)(2,1)S(1)} all-to-all(bf16[64,8,5120]{2,1,0:T(8,128)(2,1)S(1)} %pad_maximum_fusion), channel_id=1, replica_groups=mesh['dp'=8,'expert'=64] {'expert'}, dimensions={0} | all-to-all | bytes 10485760 | tf_op jit(solution)/shard_map/all_to_all | solution.py:94
  207.4 0.8 fusion.5
  208.2 0.7 copy-done.5
  208.9 0.8 fusion.11
  209.8 0.9 multiply_convert_fusion.2
  210.7 0.8 convolution_convert_fusion
  211.5 0.8 fusion.17
  212.4 0.9 add_convert_fusion
  213.3 3.1 maximum_bitcast_fusion
  216.4 14.9 %all-to-all-start.2 = ((bf16[64,8,5120]{2,1,0:T(8,128)(2,1)}), bf16[64,8,5120]{2,1,0:T(8,128)(2,1)}, u32[]{:S(2)}, u32[]{:S(2)}) async-start(bf16[64,8,5120]{2,1,0:T(8,128)(2,1)} %maximum_bitcast_fusion), calls=%async_computation.2 | async-start | bytes 10485760 | tf_op jit(solution)/shard_map/all_to_all | solution.py:101
  231.3 146.7 %all-to-all-done.2 = bf16[64,8,5120]{2,1,0:T(8,128)(2,1)} async-done(((bf16[64,8,5120]{2,1,0:T(8,128)(2,1)}), bf16[64,8,5120]{2,1,0:T(8,128)(2,1)}, u32[]{:S(2)}, u32[]{:S(2)}) %all-to-all-start.2) | async-done | bytes 5242912 | tf_op jit(solution)/shard_map/all_to_all | solution.py:101
  378.1 4.4 fusion.28
  382.4 6.0 %gather_fusion.3 = bf16[256,2560]{1,0:T(8,128)(2,1)} fusion(bf16[512,2560]{1,0:T(8,128)(2,1)} %get-tuple-element.10, s32[1024]{0:T(1024)S(1)} %pad_clamp_fusion), kind=kCustom, calls=%fused_computation.clone | custom fusion | bytes 2622464 | tf_op jit(solution)/shard_map/jit(_take)/gather | solution.py:45
  388.4 2.5 gather_fusion.4
  390.9 3.9 select_convert_fusion
  394.8 3.2 reshape.116
  398.1 4.0 convert_element_type.86
  402.0 5.3 %reduce.1 = bf16[128,2560]{1,0:T(8,128)(2,1)} reduce(bf16[128,2,2560]{2,1,0:T(2,128)(2,1)} %convert_element_type.86, bf16[]{:T(256)} %constant.21.clone.1), dimensions={1}, to_apply=%region_5.7.clone | reduce | flops 327680 | bytes 1966082 | tf_op jit(solution)/shard_map/reduce_sum | solution.py:50
  407.4 3.7 multiply_reduce_fusion
  411.1 1.2 pad_maximum_fusion.1
  412.3 7.9 %all-to-all-start.3 = ((bf16[8,16,5120]{2,1,0:T(8,128)(2,1)}), bf16[8,16,5120]{2,1,0:T(8,128)(2,1)S(1)}, u32[]{:S(2)}, u32[]{:S(2)}) async-start(bf16[8,16,5120]{2,1,0:T(8,128)(2,1)} %pad_maximum_fusion.1), calls=%async_computation.3 | async-start | bytes 2621440 | tf_op jit(solution)/shard_map/all_to_all | solution.py:108
  420.2 3.3 fusion.3
  423.5 3.6 fusion.1
  427.1 1.7 fusion.2
  428.8 19.8 %all-to-all-done.3 = bf16[8,16,5120]{2,1,0:T(8,128)(2,1)S(1)} async-done(((bf16[8,16,5120]{2,1,0:T(8,128)(2,1)}), bf16[8,16,5120]{2,1,0:T(8,128)(2,1)S(1)}, u32[]{:S(2)}, u32[]{:S(2)}) %all-to-all-start.3) | async-done | bytes 1310752 | tf_op jit(solution)/shard_map/all_to_all | solution.py:108
  448.6 0.2 reduce_sum.45
  448.9 0.7 fusion.30
  (43 shorter events, 0.5 us)
Async XLA Ops:
  0.6 209.1 %copy-start = (bf16[1,2560,128]{2,1,0:T(8,128)(2,1)S(1)}, bf16[1,2560,128]{2,1,0:T(8,128)(2,1)}, u32[]{:S(2)}) copy-start(bf16[1,2560,128]{2,1,0:T(8,128)(2,1)} %param.14) | copy-start | bytes 1966084
  45.1 2.5 copy-start.3
  48.7 158.7 %copy-start.6 = (bf16[1,128,2560]{2,1,0:T(8,128)(2,1)S(1)}, bf16[1,128,2560]{2,1,0:T(8,128)(2,1)}, u32[]{:S(2)}) copy-start(bf16[1,128,2560]{2,1,0:T(8,128)(2,1)} %param.15) | copy-start | bytes 1966084
  207.4 2.4 copy-start.2
  207.4 1.5 copy-start.5
  210.7 1.7 copy-start.9
  210.7 1.7 copy-start.7
  216.4 161.7 %all-to-all-start.2 = ((bf16[64,8,5120]{2,1,0:T(8,128)(2,1)}), bf16[64,8,5120]{2,1,0:T(8,128)(2,1)}, u32[]{:S(2)}, u32[]{:S(2)}) async-start(bf16[64,8,5120]{2,1,0:T(8,128)(2,1)} %maximum_bitcast_fusion), calls=%async_computation.2 | async-start | bytes 10485760 | tf_op jit(solution)/shard_map/all_to_all | solution.py:101
  407.4 3.7 copy-start.4
  412.3 11.2 %copy-start.10 = (bf16[512,128]{1,0:T(8,128)(2,1)S(1)}, bf16[512,128]{1,0:T(8,128)(2,1)}, u32[]{:S(2)}) copy-start(bf16[512,128]{1,0:T(8,128)(2,1)} %copy-done.9) | copy-start | bytes 393220
  412.3 36.3 %all-to-all-start.3 = ((bf16[8,16,5120]{2,1,0:T(8,128)(2,1)}), bf16[8,16,5120]{2,1,0:T(8,128)(2,1)S(1)}, u32[]{:S(2)}, u32[]{:S(2)}) async-start(bf16[8,16,5120]{2,1,0:T(8,128)(2,1)} %pad_maximum_fusion.1), calls=%async_computation.3 | async-start | bytes 2621440 | tf_op jit(solution)/shard_map/all_to_all | solution.py:108
  420.2 6.8 %slice-start = ((s8[5242880]{0:T(1024)(128)(4,1)}), s8[4194304]{0:T(1024)(128)(4,1)S(1)}, s32[]{:S(2)}) async-start(s8[5242880]{0:T(1024)(128)(4,1)} %bitcast.68), calls=%async_computation.4 | async-start | bytes 8388608
  423.5 3.6 slice-start.1
  423.5 3.6 copy-start.8
  427.0 22.5 %copy-start.1 = (bf16[1,2560,128]{2,1,0:T(8,128)(2,1)S(1)}, bf16[1,2560,128]{2,1,0:T(8,128)(2,1)}, u32[]{:S(2)}) copy-start(bf16[1,2560,128]{2,1,0:T(8,128)(2,1)} %param.14) | copy-start | bytes 1966084
